TPU v7x, 32 devices: a whole 2x2x4 slice. The times are simulated.
32 devices in a mesh: seq: 8 (over z, y), fsdp: 4 (over x, core).
Axes of the slice: x: 2, y: 2, z: 4, core: 2. Of those that a mesh axis runs over, the one named last changes fastest.
Arguments:
- inputs: bfloat16 [12288, 1536], P(('seq', 'fsdp')), may hold values from -15 to 15
- layer_norm_gain: float32 [1536], replicated, may hold values from 0.25 to 1.75
- layer_norm_bias: float32 [1536], replicated, may hold values from -4 to 4
- w_in: bfloat16 [1536, 3072], P('fsdp'), may hold values from -0.15625 to 0.15625
- dw_kernel: float32 [32, 1536], replicated, may hold values from -1 to 1
- bn_gain: float32 [1536], replicated, may hold values from 0.25 to 1.75
- bn_bias: float32 [1536], replicated, may hold values from -4 to 4
- cotangent: bfloat16 [12288, 1536], P(('seq', 'fsdp')), may hold values from -6 to 6
Outputs:
- output: bfloat16 [12288, 1536], P(('seq', 'fsdp'))
- input_gradient: bfloat16 [12288, 1536], P(('seq', 'fsdp'))
- grad_w_in: float32 [1536, 3072], P('fsdp')
- grad_kernel: float32 [32, 1536], replicated
- grad_bn_gain: float32 [1536], replicated
- grad_bn_bias: float32 [1536], replicated
- layer_norm_gain_gradient: float32 [1536], replicated
- grad_ln_bias: float32 [1536], replicated
All inputs are finite; a program needn't handle non-finite values.
Results may differ from a plain program's by a relative error of at most 0.012.
The roundings to bfloat16 on the way count: a program that leaves them out, or rounds other values in their place, can miss the bound.
Values may be sent and summed in bfloat16 or wider, within the bound.
No kernel may reach another device: no remote copies, remote signals or barrier semaphores. Data moves between devices by JAX's collectives and lax.ppermute only.
A program may use at most 128 MiB of HBM per device.

v0:
```python
import jax
import jax.numpy as jnp
from jax import lax
from jax.sharding import PartitionSpec as P

epsilon = 1e-05


def from_behind(block, axis, distance):
    devices = range(lax.axis_size(axis))
    route = [(i - distance, i) for i in devices if i - distance in devices]
    return lax.ppermute(block, axis, route)


def on_device(
    inputs, layer_norm_gain, layer_norm_bias, w_in, dw_kernel, bn_gain, bn_bias, cotangent
):
    tok_rows = inputs.shape[0]
    features = inputs.shape[1]
    kernel_len = dw_kernel.shape[0]
    all_frames = tok_rows * lax.axis_size("seq") * lax.axis_size("fsdp")
    frames = inputs.astype(jnp.float32)
    row_mean = jnp.mean(frames, axis=-1, keepdims=True)
    centered_rows = frames - row_mean
    row_inverse_deviation = lax.rsqrt(
        jnp.mean(centered_rows * centered_rows, axis=-1, keepdims=True) + epsilon
    )
    standardized_input = centered_rows * row_inverse_deviation
    normalized_rows = (standardized_input * layer_norm_gain + layer_norm_bias).astype(jnp.bfloat16)
    full_weight = lax.all_gather(w_in, "fsdp", axis=0, tiled=True)
    hidden = jnp.dot(normalized_rows, full_weight, preferred_element_type=jnp.float32)
    value_part = hidden[:, :features]
    gate_sig = jax.nn.sigmoid(hidden[:, features:])
    glu = (value_part * gate_sig).astype(jnp.bfloat16)
    past_rim = from_behind(glu[tok_rows - (kernel_len - 1) :], ("seq", "fsdp"), 1)
    padded_glu = jnp.concatenate([past_rim, glu], axis=0).astype(jnp.float32)
    conv_out = jnp.zeros((tok_rows, features), jnp.float32)
    for offset in range(kernel_len):
        conv_out = (
            conv_out
            + dw_kernel[offset]
            * padded_glu[kernel_len - 1 - offset : kernel_len - 1 - offset + tok_rows]
        )
    chan_mean = lax.psum(jnp.sum(conv_out, axis=0), ("seq", "fsdp")) / all_frames
    conv_centred = conv_out - chan_mean
    chan_var = lax.psum(jnp.sum(conv_centred * conv_centred, axis=0), ("seq", "fsdp")) / all_frames
    bn_rstd = lax.rsqrt(chan_var + epsilon)
    chat = conv_centred * bn_rstd
    z_value = chat * bn_gain + bn_bias
    z_sig = jax.nn.sigmoid(z_value)
    output = (z_value * z_sig).astype(jnp.bfloat16)
    grad_z = cotangent.astype(jnp.float32) * z_sig * (1.0 + z_value * (1.0 - z_sig))
    grad_bn_bias, grad_bn_gain = lax.psum(
        (jnp.sum(grad_z, axis=0), jnp.sum(grad_z * chat, axis=0)), ("seq", "fsdp")
    )
    grad_conv = (
        bn_gain * bn_rstd * (grad_z - grad_bn_bias / all_frames - chat * grad_bn_gain / all_frames)
    )
    future_rim = from_behind(grad_conv[: kernel_len - 1], ("seq", "fsdp"), -1)
    padded_grad = jnp.concatenate([grad_conv, future_rim], axis=0)
    grad_glu = jnp.zeros((tok_rows, features), jnp.float32)
    kernel_rows = []
    for offset in range(kernel_len):
        grad_glu = grad_glu + dw_kernel[offset] * padded_grad[offset : offset + tok_rows]
        kernel_rows.append(
            jnp.sum(
                grad_conv
                * padded_glu[kernel_len - 1 - offset : kernel_len - 1 - offset + tok_rows],
                axis=0,
            )
        )
    kernel_portion = jnp.stack(kernel_rows, axis=0)
    grad_value = grad_glu * gate_sig
    grad_gate = grad_glu * value_part * gate_sig * (1.0 - gate_sig)
    grad_hidden = jnp.concatenate([grad_value, grad_gate], axis=1).astype(jnp.bfloat16)
    normalized_gradient = lax.dot_general(
        grad_hidden, full_weight, (((1,), (1,)), ((), ())), preferred_element_type=jnp.float32
    )
    grad_kernel, layer_norm_gain_gradient, grad_ln_bias = lax.psum(
        (
            kernel_portion,
            jnp.sum(normalized_gradient * standardized_input, axis=0),
            jnp.sum(normalized_gradient, axis=0),
        ),
        ("seq", "fsdp"),
    )
    rescaled_rows = normalized_gradient * layer_norm_gain
    input_gradient = row_inverse_deviation * (
        rescaled_rows
        - jnp.mean(rescaled_rows, axis=-1, keepdims=True)
        - standardized_input * jnp.mean(rescaled_rows * standardized_input, axis=-1, keepdims=True)
    )
    row_share = lax.psum_scatter(
        lax.dot_general(
            normalized_rows,
            grad_hidden,
            (((0,), (0,)), ((), ())),
            preferred_element_type=jnp.float32,
        ),
        "fsdp",
        scatter_dimension=0,
        tiled=True,
    )
    grad_w_in = lax.psum(row_share, "seq")
    return (
        output,
        input_gradient.astype(jnp.bfloat16),
        grad_w_in,
        grad_kernel,
        grad_bn_gain,
        grad_bn_bias,
        layer_norm_gain_gradient,
        grad_ln_bias,
    )


def solution(mesh):
    placed = (
        P(("seq", "fsdp"), None),
        P(),
        P(),
        P("fsdp", None),
        P(),
        P(),
        P(),
        P(("seq", "fsdp"), None),
    )
    return jax.shard_map(
        on_device,
        mesh=mesh,
        in_specs=placed,
        out_specs=(
            P(("seq", "fsdp"), None),
            P(("seq", "fsdp"), None),
            P("fsdp", None),
            P(),
            P(),
            P(),
            P(),
            P(),
        ),
        check_vma=False,
    )
```

profile of v0, /device:TPU:0, one launch (start us, length us, event | category | flops | bytes accessed | tf_op | source)
XLA Modules:
  0.0 759.2 jit_solution(17330102155597915595)
XLA Ops:
  7.2 0.0 copy-start.10
  7.2 0.0 copy-start.2
  7.2 0.0 copy-start.11
  7.2 0.0 copy-start.12
  7.2 0.0 all-gather.2.cloned.1.call-start
  7.3 0.7 all-gather.2.cloned.1.call-update
  7.9 0.0 reduce-scatter.2.cloned.1.call-start
  8.0 0.1 copy-done.10
  8.1 0.3 slice_reduce_fusion.31
  8.4 0.2 copy-done.2
  8.6 0.2 convert_reduce_fusion
  8.8 0.4 fusion.13
  9.3 67.3 %all-gather.2.cloned.1.call-done = bf16[1536,3072]{1,0:T(8,128)(2,1)} async-done(((bf16[384,3072]{1,0:T(8,128)(2,1)}), bf16[1536,3072]{1,0:T(8,128)(2,1)}) %all-gather.2.cloned.1.call-update) | async-done | bytes 9437200 | tf_op jit(solution)/shard_map/all_gather | solution.py:30
  76.6 0.0 copy-done.11
  76.6 0.0 copy-done.12
  76.6 6.7 fusion.115
  83.2 0.0 copy-start
  83.3 0.6 multiply_convert_fusion.3
  83.9 1.5 copy-done
  85.5 2.2 collective-permute-start
  87.7 0.2 slice_reduce_fusion.30
  87.9 0.7 collective-permute-done
  88.6 0.3 maximum_convert_fusion
  88.9 10.2 %fusion.119 = (f32[1536]{0:T(1024)S(1)}, f32[384,1536]{1,0:T(8,128)}) fusion(f32[415,1536]{1,0:T(8,128)S(1)} %maximum_convert_fusion, f32[1536]{0:T(1024)S(1)} %get-tuple-element.76, f32[1536]{0:T(1024)S(1)} %get-tuple-element.77, f32[1536]{0:T(1024)S(1)} %get-tuple-element.47, f32[1536]{0:T(1024)S(1)} %get-tuple-element.48, ...), kind=kLoop, calls=%fused_computation.261 | loop fusion | flops 37747200 | bytes 78059520 | tf_op jit(solution)/shard_map/reduce_sum | solution.py:44
  99.1 44.0 %psum.56 = f32[1536]{0:T(1024)S(1)} all-reduce(f32[1536]{0:T(1024)S(1)} %get-tuple-element.85), channel_id=1, replica_groups=mesh['seq'=8,'fsdp'=4] {'seq','fsdp'}, use_global_device_ids=true, to_apply=%region_3.0 | all-reduce | flops 1536 | bytes 12288 | tf_op jit(solution)/shard_map/psum | solution.py:44
  143.2 1.9 multiply_reduce_fusion.33
  145.1 40.1 %psum.57 = f32[1536]{0:T(1024)S(1)} all-reduce(f32[1536]{0:T(1024)S(1)} %multiply_reduce_fusion.33), channel_id=1, replica_groups=mesh['seq'=8,'fsdp'=4] {'seq','fsdp'}, use_global_device_ids=true, to_apply=%region_5.0 | all-reduce | flops 1536 | bytes 12288 | tf_op jit(solution)/shard_map/psum | solution.py:46
  185.2 0.0 copy-done.13
  185.2 0.0 copy-done.14
  185.3 4.5 fusion.117
  189.7 40.2 %all-reduce.1 = (f32[1536]{0:T(1024)S(1)}, f32[1536]{0:T(1024)S(1)}) all-reduce(f32[1536]{0:T(1024)S(1)} %get-tuple-element.41, f32[1536]{0:T(1024)S(1)} %get-tuple-element.40), channel_id=1, replica_groups=mesh['seq'=8,'fsdp'=4] {'seq','fsdp'}, use_global_device_ids=true, to_apply=%region_9.0 | all-reduce | flops 3072 | bytes 24576 | tf_op jit(solution)/shard_map/psum | solution.py:53
  230.0 0.6 copy-done.16
  230.5 8.2 %multiply_reduce_fusion = (f32[1536]{0:T(1024)S(1)}, f32[1536]{0:T(1024)S(1)}, f32[1536]{0:T(1024)S(1)}, f32[1536]{0:T(1024)S(1)}, f32[1536]{0:T(1024)S(1)}, /*i...) fusion(f32[415,1536]{1,0:T(8,128)S(1)} %maximum_convert_fusion,, ...), kind=kLoop, calls=%fused_computation.169 | loop fusion | flops 31822848 | bytes 48519168 | tf_op jit(solution)/shard_map/reduce_sum | solution.py:66
  238.8 0.0 copy-done.15
  238.8 0.0 copy-start.1
  238.8 1.4 copy-done.1
  240.2 1.5 collective-permute-start.1
  241.7 1.9 collective-permute-done.1
  243.5 40.4 %multiply_convert_fusion.1 = (bf16[384,1536]{1,0:T(8,128)(2,1)S(1)}, f32[384,1536]{1,0:T(8,128)}) fusion(f32[384,3072]{1,0:T(8,128)} %copy-done, f32[31,1536]{1,0:T(8,128)S(1)} %collective-permute-done.1, f32[384,1536]{1,0:T(8,128)} %copy-done.1, f32[1536]{0:T(1024)S(1)} %get-tuple-element.76, f32[1536]{0:T(1024)S(1)} %get-tuple-element.77, ...), kind=kLoop, calls=%fused_computation.202 | loop fusion | flops 58392576 | bytes 8644608 | tf_op jit(solution)/shard_map/convert
  283.9 0.0 copy-start.3
  284.0 4.4 multiply_convert_fusion
  288.4 0.0 copy-start.7
  288.4 0.0 copy-done.5
  288.4 1.0 copy-done.7
  289.4 9.4 %fusion.109 = f32[1536,3072]{1,0:T(8,128)} fusion(bf16[384,1536]{1,0:T(8,128)(2,1)S(1)} %multiply_convert_fusion, bf16[384,1536]{1,0:T(8,128)(2,1)S(1)} %get-tuple-element.83, bf16[384,1536]{1,0:T(8,128)(2,1)S(1)} %copy-done.3, f32[1536]{0:T(1024)S(1)} %copy-done.12, f32[1536]{0:T(1024)S(1)} %copy-done.11, f32[384]{0:T(512)S(1)} %add_rsqrt_fusion.1, ...), kind=kOutput, calls=%fused_computation.214 | convolution fusion | flops 3632136192 | bytes 22428672 | tf_op jit(solution)/shard_map/dot_general | solution.py:94
  298.8 0.0 reduce-scatter.2.cloned.1.call-update
  298.8 0.0 all-reduce.7.cloned.1.call-start
  298.9 5.4 multiply_reduce_fusion.18
  304.8 2.8 stack.131
  307.6 0.0 all-reduce.7.cloned.1.call-update
  307.6 0.3 all-reduce.5.cloned.1.call-start
  307.9 134.5 %reduce-scatter.2.cloned.1.call-done = f32[384,3072]{1,0:T(8,128)} async-done(((f32[1536,3072]{1,0:T(8,128)}), f32[384,3072]{1,0:T(8,128)}) %reduce-scatter.2.cloned.1.call-update) | async-done | bytes 4718608 | tf_op jit(solution)/shard_map/reduce_scatter | solution.py:93
  442.4 0.0 all-reduce.5.cloned.1.call-update
  442.4 1.2 copy-done.4
  443.6 0.4 copy-done.6
  444.0 0.4 copy-done.8
  444.3 10.0 %fusion.12 = (f32[1536]{0:T(1024)}, f32[384]{0:T(512)}, f32[384]{0:T(512)}, f32[1536]{0:T(1024)}, f32[384,1536]{1,0:T(8,128)}) fusion(bf16[384,1536]{1,0:T(8,128)(2,1)S(1)} %copy-done.4, f32[384]{0:T(512)S(1)} %add_rsqrt_fusion.1, f32[384]{0:T(512)S(1)} %broadcast_multiply_fusion.4, f32[1536]{0:T(1024)S(1)} %copy-done.11, ...), kind=kOutput, calls=%fused_computation.44 | convolution fusion | flops 3634491392 | bytes 15360000 | tf_op jit(solution)/shard_map/dot_general | solution.py:76
  454.3 39.7 %all-reduce = (f32[1536]{0:T(1024)}, f32[1536]{0:T(1024)}) all-reduce(f32[1536]{0:T(1024)} %get-tuple-element.42, f32[1536]{0:T(1024)} %get-tuple-element.45), channel_id=1, replica_groups=mesh['seq'=8,'fsdp'=4] {'seq','fsdp'}, use_global_device_ids=true, to_apply=%region_48.0 | all-reduce | flops 3072 | bytes 24576 | tf_op jit(solution)/shard_map/psum | solution.py:79
  494.0 0.7 broadcast_multiply_fusion.2
  494.7 3.4 fusion.11
  498.1 74.3 %all-reduce.7.cloned.1.call-done = f32[32,1536]{1,0:T(8,128)} async-done(((f32[32,1536]{1,0:T(8,128)}), f32[32,1536]{1,0:T(8,128)}) %all-reduce.7.cloned.1.call-update) | async-done | bytes 196624 | tf_op jit(solution)/shard_map/psum | solution.py:79
  572.4 174.5 %all-reduce.5.cloned.1.call-done = f32[384,3072]{1,0:T(8,128)} async-done(((f32[384,3072]{1,0:T(8,128)}), f32[384,3072]{1,0:T(8,128)}) %all-reduce.5.cloned.1.call-update) | async-done | bytes 4718608 | tf_op jit(solution)/shard_map/psum | solution.py:104
  746.9 5.1 copy.18
  752.0 0.7 copy.19
  (50 shorter events, 0.3 us)
Async XLA Ops:
  7.2 0.9 copy-start.10
  7.2 1.4 copy-start.2
  7.2 69.4 %copy-start.11 = (f32[1536]{0:T(1024)S(1)}, f32[1536]{0:T(1024)}, u32[]{:S(2)}) copy-start(f32[1536]{0:T(1024)} %param.9) | copy-start | bytes 18436
  7.2 69.4 %copy-start.12 = (f32[1536]{0:T(1024)S(1)}, f32[1536]{0:T(1024)}, u32[]{:S(2)}) copy-start(f32[1536]{0:T(1024)} %param.10) | copy-start | bytes 18436
  7.2 69.4 %all-gather.2.cloned.1.call-start = ((), (), s32[]{:S(2)}) async-start(), calls=%async_computation.1 | async-start | bytes 11796480 | tf_op jit(solution)/shard_map/all_gather | solution.py:30
  7.9 434.4 %reduce-scatter.2.cloned.1.call-start = ((), (), s32[]{:S(2)}) async-start(), calls=%async_computation.2 | async-start | bytes 23592960 | tf_op jit(solution)/shard_map/reduce_scatter | solution.py:93
  83.2 2.2 copy-start
  85.5 3.1 collective-permute-start
  99.1 86.1 %copy-start.13 = (f32[1536]{0:T(1024)S(1)}, f32[1536]{0:T(1024)}, u32[]{:S(2)}) copy-start(f32[1536]{0:T(1024)} %param.13) | copy-start | bytes 18436
  99.1 86.1 %copy-start.14 = (f32[1536]{0:T(1024)S(1)}, f32[1536]{0:T(1024)}, u32[]{:S(2)}) copy-start(f32[1536]{0:T(1024)} %param.14) | copy-start | bytes 18436
  229.9 0.6 copy-start.16
  229.9 8.9 %copy-start.15 = (f32[1536]{0:T(1024)}, f32[1536]{0:T(1024)S(1)}, u32[]{:S(2)}) copy-start(f32[1536]{0:T(1024)S(1)} %get-tuple-element.97) | copy-start | bytes 18436
  238.8 1.4 copy-start.1
  240.2 3.3 collective-permute-start.1
  283.9 4.5 copy-start.5
  283.9 5.5 copy-start.3
  288.4 1.0 copy-start.7
  298.8 273.6 %all-reduce.7.cloned.1.call-start = ((), (), s32[]{:S(2)}) async-start(), calls=%async_computation.4 | async-start | bytes 393216 | tf_op jit(solution)/shard_map/psum | solution.py:79
  307.6 439.3 %all-reduce.5.cloned.1.call-start = ((), (), s32[]{:S(2)}) async-start(), calls=%async_computation.3 | async-start | bytes 9437184 | tf_op jit(solution)/shard_map/psum | solution.py:104
  442.4 1.3 copy-start.4
  442.4 1.6 copy-start.6
  442.4 2.0 copy-start.8
  746.9 5.1 copy-start.9
Sparse Core Ops, SparseCore 0:
  9.6 66.9 all-gather.1
  298.9 143.3 reduce-scatter.1
  449.4 122.9 all-reduce.6
  576.3 170.5 all-reduce.4
where the time goes:
time: 760 us; the launch traced here: 759 us
  waiting for transfers between devices  454 us (60%)
  blocking collectives  164 us (22%)
  other arithmetic  80.9 us (11%)
  matrix products  26 us (3%)
  local copies, waits for them, and re-layouts  16.1 us (2%)
  between operations  14.2 us (2%)
    psum x1, waiting for transfers between devices, on_device(): grad_w_in = lax.psum(row_share, 'seq')  174 us
    reduce_scatter x1, waiting for transfers between devices, on_device(): lax.psum_scatter(lax.dot_general(normalized_rows, grad_hidden, (((0,), (0...  135 us
    psum x1, waiting for transfers between devices, on_device(): lax.psum((kernel_portion, jnp.sum(normalized_gradient * standardized_inpu...  74.3 us
    all_gather x1, waiting for transfers between devices, on_device(): full_weight = lax.all_gather(w_in, 'fsdp', axis=0, tiled=True)  67.3 us
    another operation x2, other arithmetic  44.8 us
    psum x1, blocking collectives, on_device(): lax.psum(jnp.sum(conv_out, axis=0), ('seq', 'fsdp')) / all_frames  44 us
    psum x1, blocking collectives, on_device(): lax.psum((jnp.sum(grad_z, axis=0), jnp.sum(grad_z * chat, axis=0)), ('seq...  40.2 us
    psum x1, blocking collectives, on_device(): lax.psum(jnp.sum(conv_centred * conv_centred, axis=0), ('seq', 'fsdp'))  40.1 us
  transfers between devices with their start and end apart: 6, of which 6 were waited for; matrix products, arithmetic and copies ran while one was open for 3% of the time, Pallas kernels for 0%

commit v1 on v0

--- a/solution.py
+++ b/solution.py
@@ -27,7 +27,12 @@
     )
     standardized_input = centered_rows * row_inverse_deviation
     normalized_rows = (standardized_input * layer_norm_gain + layer_norm_bias).astype(jnp.bfloat16)
-    full_weight = lax.all_gather(w_in, "fsdp", axis=0, tiled=True)
+    ring = [w_in]
+    for hop in range(3):
+        ring.append(lax.ppermute(ring[-1], "fsdp", [(dev, (dev + 1) % 4) for dev in range(4)]))
+    full_weight = jnp.roll(
+        jnp.concatenate(ring[::-1], axis=0), (lax.axis_index("fsdp") + 1) * ring[0].shape[0], axis=0
+    )
     hidden = jnp.dot(normalized_rows, full_weight, preferred_element_type=jnp.float32)
     value_part = hidden[:, :features]
     gate_sig = jax.nn.sigmoid(hidden[:, features:])

time: 760 us -> 710 us (0.934)
  waiting for transfers between devices: 454 us -> 386 us
  local copies, waits for them, and re-layouts: 16.1 us -> 31.4 us
    ppermute x0 -> x3, waiting for transfers between devices: none -> 80.6 us  [on_device(): lax.ppermute(ring[-1], 'fsdp', [(dev, (dev + 1) % 4) for dev in range(4)])]
    psum x1, waiting for transfers between devices: 74.3 us -> 0.01 us  [on_device(): lax.psum((kernel_portion, jnp.sum(normalized_gradient * standardized_inpu...]
    all_gather x1 -> x0, waiting for transfers between devices: 67.3 us -> none  [on_device(): full_weight = lax.all_gather(w_in, 'fsdp', axis=0, tiled=True)]
    unnamed x36 -> x45, local copies, waits for them, and re-layouts: 12.5 us -> 24.9 us
  transfers between devices with their start and end apart: 6 -> 8, of which waited for: 6 -> 6; matrix products, arithmetic and copies ran while one was open for 3% -> 4% of each run, Pallas kernels for 0% -> 0%
where the time goes in v1:
time: 710 us; the launch traced here: 709 us
  waiting for transfers between devices  386 us (54%)
  blocking collectives  165 us (23%)
  other arithmetic  83.2 us (12%)
  local copies, waits for them, and re-layouts  31.4 us (4%)
  matrix products  23.6 us (3%)
  between operations  16 us (2%)
    psum x1, waiting for transfers between devices, on_device(): grad_w_in = lax.psum(row_share, 'seq')  168 us
    reduce_scatter x1, waiting for transfers between devices, on_device(): lax.psum_scatter(lax.dot_general(normalized_rows, grad_hidden, (((0,), (0...  135 us
    ppermute x3, waiting for transfers between devices, on_device(): lax.ppermute(ring[-1], 'fsdp', [(dev, (dev + 1) % 4) for dev in range(4)])  80.6 us
    psum x1, blocking collectives, on_device(): lax.psum(jnp.sum(conv_out, axis=0), ('seq', 'fsdp')) / all_frames  44.6 us
    another operation x2, other arithmetic  44.6 us
    psum x1, blocking collectives, on_device(): lax.psum(jnp.sum(conv_centred * conv_centred, axis=0), ('seq', 'fsdp'))  40.6 us
    psum x1, blocking collectives, on_device(): lax.psum((jnp.sum(grad_z, axis=0), jnp.sum(grad_z * chat, axis=0)), ('seq...  39.8 us
    psum x1, blocking collectives, on_device(): lax.psum((kernel_portion, jnp.sum(normalized_gradient * standardized_inpu...  39.7 us
  transfers between devices with their start and end apart: 8, of which 6 were waited for; matrix products, arithmetic and copies ran while one was open for 4% of the time, Pallas kernels for 0%

profile of v1, /device:TPU:0, one launch (start us, length us, event | category | flops | bytes accessed | tf_op | source)
XLA Modules:
  0.0 708.8 jit_solution(8734003535897168089)
XLA Ops:
  8.0 0.0 reduce-scatter.2.cloned.1.call-start
  8.0 0.5 collective-permute-start
  8.5 28.7 %collective-permute-done = bf16[384,3072]{1,0:T(8,128)(2,1)S(1)} collective-permute-done((bf16[384,3072]{1,0:T(8,128)(2,1)}, bf16[384,3072]{1,0:T(8,128)(2,1)S(1)}, u32[]{:S(2)}, u32[]{:S(2)}) %collective-permute-start) | collective-permute-done | bytes 2359328 | tf_op jit(solution)/shard_map/ppermute | solution.py:32
  37.2 0.0 collective-permute-start.1
  37.3 28.3 %collective-permute-done.1 = bf16[384,3072]{1,0:T(8,128)(2,1)} collective-permute-done((bf16[384,3072]{1,0:T(8,128)(2,1)S(1)}, bf16[384,3072]{1,0:T(8,128)(2,1)}, u32[]{:S(2)}, u32[]{:S(2)}) %collective-permute-start.1) | collective-permute-done | bytes 2359328 | tf_op jit(solution)/shard_map/ppermute | solution.py:32
  65.6 1.8 slice_reduce_fusion.31
  67.4 1.5 convert_reduce_fusion
  68.9 1.7 fusion.17
  70.6 23.6 %collective-permute-done.2 = bf16[384,3072]{1,0:T(8,128)(2,1)} collective-permute-done((bf16[384,3072]{1,0:T(8,128)(2,1)}, bf16[384,3072]{1,0:T(8,128)(2,1)}, u32[]{:S(2)}, u32[]{:S(2)}) %collective-permute-start.2) | collective-permute-done | bytes 2359328 | tf_op jit(solution)/shard_map/ppermute | solution.py:32
  94.2 1.8 constant_dynamic-update-slice_fusion.7
  96.0 1.8 constant_dynamic-update-slice_fusion.6
  97.8 0.0 copy-start.5
  97.8 0.2 constant_dynamic-update-slice_fusion.5
  98.0 1.5 copy-done.5
  99.5 0.2 constant_dynamic-update-slice_fusion.4
  99.6 1.8 constant_dynamic-update-slice_fusion.3
  101.5 1.8 constant_dynamic-update-slice_fusion.2
  103.3 0.2 constant_dynamic-update-slice_fusion.1
  103.4 0.0 copy-start.2
  103.5 0.0 copy-start.12
  103.5 0.0 copy-start.13
  103.5 0.2 constant_dynamic-update-slice_fusion
  103.6 1.1 copy-done.2
  104.7 4.2 fusion.2
  108.9 2.3 copy-done.10
  111.2 0.6 multiply_convert_fusion.3
  111.8 1.6 copy-done
  113.4 1.8 collective-permute-start.3
  115.3 1.6 slice_reduce_fusion.30
  116.8 0.3 maximum_convert_fusion
  117.2 10.2 %fusion.123 = (f32[1536]{0:T(1024)S(1)}, f32[384,1536]{1,0:T(8,128)}) fusion(f32[415,1536]{1,0:T(8,128)S(1)} %maximum_convert_fusion, f32[1536]{0:T(1024)S(1)} %get-tuple-element.76, f32[1536]{0:T(1024)S(1)} %get-tuple-element.77, f32[1536]{0:T(1024)S(1)} %get-tuple-element.47, f32[1536]{0:T(1024)S(1)} %get-tuple-element.48, ...), kind=kLoop, calls=%fused_computation.273 | loop fusion | flops 37747200 | bytes 78059520 | tf_op jit(solution)/shard_map/reduce_sum | solution.py:49
  127.4 44.6 %psum.56 = f32[1536]{0:T(1024)S(1)} all-reduce(f32[1536]{0:T(1024)S(1)} %get-tuple-element.85), channel_id=1, replica_groups=mesh['seq'=8,'fsdp'=4] {'seq','fsdp'}, use_global_device_ids=true, to_apply=%region_3.4 | all-reduce | flops 1536 | bytes 12288 | tf_op jit(solution)/shard_map/psum | solution.py:49
  172.0 1.9 multiply_reduce_fusion.33
  173.9 40.6 %psum.57 = f32[1536]{0:T(1024)S(1)} all-reduce(f32[1536]{0:T(1024)S(1)} %multiply_reduce_fusion.33), channel_id=1, replica_groups=mesh['seq'=8,'fsdp'=4] {'seq','fsdp'}, use_global_device_ids=true, to_apply=%region_5.6 | all-reduce | flops 1536 | bytes 12288 | tf_op jit(solution)/shard_map/psum | solution.py:51
  214.5 4.5 fusion.121
  219.0 39.8 %all-reduce.1 = (f32[1536]{0:T(1024)S(1)}, f32[1536]{0:T(1024)S(1)}) all-reduce(f32[1536]{0:T(1024)S(1)} %get-tuple-element.41, f32[1536]{0:T(1024)S(1)} %get-tuple-element.40), channel_id=1, replica_groups=mesh['seq'=8,'fsdp'=4] {'seq','fsdp'}, use_global_device_ids=true, to_apply=%region_9.10 | all-reduce | flops 3072 | bytes 24576 | tf_op jit(solution)/shard_map/psum | solution.py:58
  258.8 0.6 copy-done.17
  259.4 8.2 %multiply_reduce_fusion = (f32[1536]{0:T(1024)S(1)}, f32[1536]{0:T(1024)S(1)}, f32[1536]{0:T(1024)S(1)}, f32[1536]{0:T(1024)S(1)}, f32[1536]{0:T(1024)S(1)}, /*i...) fusion(f32[415,1536]{1,0:T(8,128)S(1)} %maximum_convert_fusion,, ...), kind=kLoop, calls=%fused_computation.173 | loop fusion | flops 31822848 | bytes 48519168 | tf_op jit(solution)/shard_map/reduce_sum | solution.py:71
  267.7 1.4 copy-done.1
  269.1 1.3 collective-permute-start.4
  270.4 2.0 collective-permute-done.4
  272.5 40.1 %multiply_convert_fusion.1 = (bf16[384,1536]{1,0:T(8,128)(2,1)S(1)}, f32[384,1536]{1,0:T(8,128)}) fusion(f32[384,3072]{1,0:T(8,128)} %copy-done, f32[31,1536]{1,0:T(8,128)S(1)} %collective-permute-done.4, f32[384,1536]{1,0:T(8,128)} %copy-done.1, f32[1536]{0:T(1024)S(1)} %get-tuple-element.76, f32[1536]{0:T(1024)S(1)} %get-tuple-element.77, ...), kind=kLoop, calls=%fused_computation.206 | loop fusion | flops 58392576 | bytes 8644608 | tf_op jit(solution)/shard_map/convert
  312.6 0.0 copy-start.3
  312.6 4.4 multiply_convert_fusion
  317.1 1.0 copy-done.8
  318.1 9.3 %fusion.113 = f32[1536,3072]{1,0:T(8,128)} fusion(bf16[384,1536]{1,0:T(8,128)(2,1)S(1)} %multiply_convert_fusion, bf16[384,1536]{1,0:T(8,128)(2,1)S(1)} %get-tuple-element.83, bf16[384,1536]{1,0:T(8,128)(2,1)S(1)} %copy-done.3, f32[1536]{0:T(1024)S(1)} %copy-done.13, f32[1536]{0:T(1024)S(1)} %copy-done.12, f32[384]{0:T(512)S(1)} %add_rsqrt_fusion.1, ...), kind=kOutput, calls=%fused_computation.218 | convolution fusion | flops 3632136192 | bytes 22428672 | tf_op jit(solution)/shard_map/dot_general | solution.py:99
  327.4 0.0 reduce-scatter.2.cloned.1.call-update
  327.5 0.3 all-reduce.7.cloned.1.call-start
  327.7 5.4 multiply_reduce_fusion.18
  333.6 2.8 stack.131
  336.4 0.0 all-reduce.7.cloned.1.call-update
  336.4 0.0 all-reduce.5.cloned.1.call-start
  336.5 135.1 %reduce-scatter.2.cloned.1.call-done = f32[384,3072]{1,0:T(8,128)} async-done(((f32[1536,3072]{1,0:T(8,128)}), f32[384,3072]{1,0:T(8,128)}) %reduce-scatter.2.cloned.1.call-update) | async-done | bytes 4718608 | tf_op jit(solution)/shard_map/reduce_scatter | solution.py:98
  471.6 0.0 all-reduce.5.cloned.1.call-update
  471.7 1.2 copy-done.4
  472.9 0.4 copy-done.7
  473.3 0.4 copy-done.9
  473.6 10.0 %fusion.16 = (f32[1536]{0:T(1024)}, f32[384]{0:T(512)}, f32[384]{0:T(512)}, f32[1536]{0:T(1024)}, f32[384,1536]{1,0:T(8,128)}) fusion(bf16[384,1536]{1,0:T(8,128)(2,1)S(1)} %copy-done.4, f32[384]{0:T(512)S(1)} %add_rsqrt_fusion.1, f32[384]{0:T(512)S(1)} %broadcast_multiply_fusion.4, f32[1536]{0:T(1024)S(1)} %copy-done.12, ...), kind=kOutput, calls=%fused_computation.48 | convolution fusion | flops 3634491392 | bytes 15360004 | tf_op jit(solution)/shard_map/dot_general | solution.py:81
  483.6 39.7 %all-reduce = (f32[1536]{0:T(1024)}, f32[1536]{0:T(1024)}) all-reduce(f32[1536]{0:T(1024)} %get-tuple-element.42, f32[1536]{0:T(1024)} %get-tuple-element.45), channel_id=1, replica_groups=mesh['seq'=8,'fsdp'=4] {'seq','fsdp'}, use_global_device_ids=true, to_apply=%region_48.49 | all-reduce | flops 3072 | bytes 24576 | tf_op jit(solution)/shard_map/psum | solution.py:84
  523.3 0.7 broadcast_multiply_fusion.2
  524.0 3.4 fusion.15
  527.5 168.2 %all-reduce.5.cloned.1.call-done = f32[384,3072]{1,0:T(8,128)} async-done(((f32[384,3072]{1,0:T(8,128)}), f32[384,3072]{1,0:T(8,128)}) %all-reduce.5.cloned.1.call-update) | async-done | bytes 4718608 | tf_op jit(solution)/shard_map/psum | solution.py:109
  695.6 5.1 copy.25
  700.7 0.7 copy.26
  (63 shorter events, 0.3 us)
Async XLA Ops:
  8.0 463.6 %reduce-scatter.2.cloned.1.call-start = ((), (), s32[]{:S(2)}) async-start(), calls=%async_computation.1 | async-start | bytes 23592960 | tf_op jit(solution)/shard_map/reduce_scatter | solution.py:98
  8.0 29.2 %collective-permute-start = (bf16[384,3072]{1,0:T(8,128)(2,1)}, bf16[384,3072]{1,0:T(8,128)(2,1)S(1)}, u32[]{:S(2)}, u32[]{:S(2)}) collective-permute-start(bf16[384,3072]{1,0:T(8,128)(2,1)} %param.11), channel_id=1, source_target_pairs={{0,1},{1,2},{2,3},{3,0},{4,5},{5,6},{6,7},{7,4},{8,9},{9,10},{10,1... | collective-permute-start | bytes 7077896 | tf_op jit(solution)/shard_map/ppermute | solution.py:32
  37.2 28.4 %collective-permute-start.1 = (bf16[384,3072]{1,0:T(8,128)(2,1)S(1)}, bf16[384,3072]{1,0:T(8,128)(2,1)}, u32[]{:S(2)}, u32[]{:S(2)}) collective-permute-start(bf16[384,3072]{1,0:T(8,128)(2,1)S(1)} %collective-permute-done), channel_id=1, source_target_pairs={{0,1},{1,2},{2,3},{3,0},{4,5},{5,6},{6,7},{7,4},{8,9},{9,10},{10,1... | collective-permute-start | bytes 7077896 | tf_op jit(solution)/shard_map/ppermute | solution.py:32
  65.6 28.6 %collective-permute-start.2 = (bf16[384,3072]{1,0:T(8,128)(2,1)}, bf16[384,3072]{1,0:T(8,128)(2,1)}, u32[]{:S(2)}, u32[]{:S(2)}) collective-permute-start(bf16[384,3072]{1,0:T(8,128)(2,1)} %collective-permute-done.1), channel_id=1, source_target_pairs={{0,1},{1,2},{2,3},{3,0},{4,5},{5,6},{6,7},{7,4},{8,9},{9,10},{10,1... | collective-permute-start | bytes 7077896 | tf_op jit(solution)/shard_map/ppermute | solution.py:32
  97.8 1.7 copy-start.5
  103.4 1.3 copy-start.2
  103.5 1.3 copy-start.12
  103.5 1.3 copy-start.13
  104.7 6.5 copy-start.10
  111.2 2.2 copy-start
  113.4 3.4 collective-permute-start.3
  127.4 87.1 %copy-start.14 = (f32[1536]{0:T(1024)S(1)}, f32[1536]{0:T(1024)}, u32[]{:S(2)}) copy-start(f32[1536]{0:T(1024)} %param.13) | copy-start | bytes 18436
  127.4 87.1 %copy-start.15 = (f32[1536]{0:T(1024)S(1)}, f32[1536]{0:T(1024)}, u32[]{:S(2)}) copy-start(f32[1536]{0:T(1024)} %param.14) | copy-start | bytes 18436
  258.8 0.6 copy-start.17
  258.8 8.9 %copy-start.16 = (f32[1536]{0:T(1024)}, f32[1536]{0:T(1024)S(1)}, u32[]{:S(2)}) copy-start(f32[1536]{0:T(1024)S(1)} %get-tuple-element.97) | copy-start | bytes 18436
  267.7 1.4 copy-start.1
  269.1 3.3 collective-permute-start.4
  312.6 4.5 copy-start.6
  312.6 5.5 copy-start.3
  317.1 1.0 copy-start.8
  327.5 200.0 %all-reduce.7.cloned.1.call-start = ((), (), s32[]{:S(2)}) async-start(), calls=%async_computation.3 | async-start | bytes 393216 | tf_op jit(solution)/shard_map/psum | solution.py:84
  336.4 359.2 %all-reduce.5.cloned.1.call-start = ((), (), s32[]{:S(2)}) async-start(), calls=%async_computation.2 | async-start | bytes 9437184 | tf_op jit(solution)/shard_map/psum | solution.py:109
  471.6 1.3 copy-start.4
  471.6 1.6 copy-start.7
  471.6 2.0 copy-start.9
  695.6 5.1 copy-start.11
Sparse Core Ops, SparseCore 0:
  327.6 144.0 reduce-scatter.1
Sparse Core Ops, SparseCore 1:
  336.5 185.0 all-reduce.6
  525.5 170.0 all-reduce.4
